TPU v7x, 32 devices: a whole 2x2x4 slice. The times are simulated.
32 devices in a mesh: groups: 2 (over y), tm: 4 (over z), mp: 2 (over x), section: 2 (over core).
Axes of the slice: x: 2, y: 2, z: 4, core: 2. Of those that a mesh axis runs over, the one named last changes fastest.
Arguments:
- series: bfloat16 [4, 64, 16384], P('groups', None, 'tm'), parts along dimension 0, may hold values from -80 to 80
- lengths: int32 [4], P('groups'), parts along dimension 0, may hold values from 2048 to 16384, as said below
- patch_weight: bfloat16 [4096, 1280], P(None, ('mp', 'section')), may hold values from -0.09375 to 0.09375
- norm_gain: bfloat16 [2, 1280], P('section'), may hold values from 0.099609375 to 1.8984375
- query_weight: bfloat16 [2, 1280, 1280], P('section', None, 'mp'), may hold values from -4 to 4
- key_weight: bfloat16 [2, 1280, 320], P('section', None, 'mp'), may hold values from -4 to 4
- value_weight: bfloat16 [2, 1280, 320], P('section', None, 'mp'), may hold values from -0.15625 to 0.15625
- out_weight: bfloat16 [2, 1280, 1280], P('section', 'mp'), may hold values from -0.625 to 0.625
Outputs:
- key_cache: bfloat16 [2, 4, 4, 80, 512], P('section', 'groups', 'mp', None, 'tm'), parts along dimension 1
- value_cache: bfloat16 [2, 4, 4, 80, 512], P('section', 'groups', 'mp', None, 'tm'), parts along dimension 1
- hidden: bfloat16 [4, 512, 1280], P(('groups', 'section'), 'tm', 'mp'), parts along dimension 0
There are 2 independent parts, one for each index of `groups`. A program takes and returns all parts, laid end to end along the dimension named above; an argument that names none is the same for every part. Nothing has to cross between parts.
Inputs may be any that keep to these rules, and one draw needn't show every extreme that they name: `lengths`: a multiple of 32; the last sequence of a part has its whole history of 16384 steps.
All inputs are finite; a program needn't handle non-finite values.
Results may differ from a plain program's by a relative error of at most 0.02.
Values may be sent and summed in bfloat16 or wider, within the bound.
No kernel may reach another device: no remote copies, remote signals or barrier semaphores. Data moves between devices by JAX's collectives and lax.ppermute only.
A program may use at most 64 MiB of HBM per device.

v0:
```python
import jax
import jax.numpy as jnp
from jax import lax
from jax.sharding import PartitionSpec as P

STRIDE = 32
HD = 80


def from_behind(value, axis, by):
    size = lax.axis_size(axis)
    pairs = [(i, i + by) for i in range(size) if 0 <= i + by < size]
    return lax.ppermute(value, axis, pairs)


def from_root(value, axis, root):
    mine = lax.axis_index(axis) == root
    return lax.psum(jnp.where(mine, value, jnp.zeros_like(value)), axis)


def absorb_block(running, key_block, value_block, key_start, query_rows, query_pos, first_valid):
    run_max, run_sum, accumulated = running
    key_pos = key_start + jnp.arange(key_block.shape[3], dtype=jnp.int32)
    allowed = (key_pos[None, None, :] <= query_pos[None, :, None]) & (
        (key_pos[None, None, :] >= first_valid[:, None, None])
        | (key_pos[None, None, :] == query_pos[None, :, None])
    )
    scores = jnp.einsum(
        "btkgh,bkhn->bkgtn", query_rows, key_block, preferred_element_type=jnp.float32
    )
    scores = jnp.where(allowed[:, None, None], scores, -jnp.inf)
    new_max = jnp.maximum(run_max, jnp.max(scores, -1))
    rescale = jnp.exp(run_max - new_max)
    exp_scores = jnp.exp(scores - new_max[..., None])
    new_sum = run_sum * rescale + jnp.sum(exp_scores, -1)
    contribution = jnp.einsum(
        "bkgtn,bkhn->bkgth",
        exp_scores.astype(jnp.bfloat16),
        value_block,
        preferred_element_type=jnp.float32,
    )
    return (new_max, new_sum, accumulated * rescale[..., None] + contribution)


def attend_layer(
    hidden_in, seq_lens, gain, query_w, key_w, value_w, out_w, tok_start, total_tokens
):
    batch_count, tok_count, share_width = hidden_in.shape
    hidden32 = hidden_in.astype(jnp.float32)
    gain32 = gain.astype(jnp.float32)
    scaled = hidden32 * lax.rsqrt(jnp.mean(hidden32 * hidden32, -1, keepdims=True) + 1e-06)
    layer_input = (scaled * gain32).astype(jnp.bfloat16)
    queries = (
        jnp.einsum("btd,de->bte", layer_input, query_w, preferred_element_type=jnp.float32)
        * HD ** (-0.5)
    ).astype(jnp.bfloat16)
    key_t = jnp.einsum(
        "btd,de->bet", layer_input, key_w, preferred_element_type=jnp.float32
    ).astype(jnp.bfloat16)
    value_t = jnp.einsum(
        "btd,de->bet", layer_input, value_w, preferred_element_type=jnp.float32
    ).astype(jnp.bfloat16)
    kv_local = key_w.shape[1] // HD
    group_size = query_w.shape[1] // key_w.shape[1]
    key_t = key_t.reshape(batch_count, kv_local, HD, tok_count)
    value_t = value_t.reshape(batch_count, kv_local, HD, tok_count)
    query_rows = queries.reshape(batch_count, tok_count, kv_local, group_size, HD)
    query_pos = tok_start + jnp.arange(tok_count, dtype=jnp.int32)
    first_valid = total_tokens - seq_lens // STRIDE
    start_state = (
        jnp.full((batch_count, kv_local, group_size, tok_count), -1e30, jnp.float32),
        jnp.zeros((batch_count, kv_local, group_size, tok_count), jnp.float32),
        jnp.zeros((batch_count, kv_local, group_size, tok_count, HD), jnp.float32),
    )
    key_piece = lax.all_gather(key_t, "tm", axis=3, tiled=True)
    value_piece = lax.all_gather(value_t, "tm", axis=3, tiled=True)
    key_count = key_piece.shape[3]
    block_width = 1024 if key_count % 1024 == 0 else key_count
    rounds = key_count // block_width
    key_blocks = jnp.moveaxis(
        key_piece.reshape(batch_count, kv_local, HD, rounds, block_width), 3, 0
    )
    value_blocks = jnp.moveaxis(
        value_piece.reshape(batch_count, kv_local, HD, rounds, block_width), 3, 0
    )
    offsets = jnp.arange(rounds, dtype=jnp.int32) * block_width

    def scan_step(state, block_item):
        key_block, value_block, offset = block_item
        return (
            absorb_block(state, key_block, value_block, offset, query_rows, query_pos, first_valid),
            None,
        )

    result, _ = lax.scan(scan_step, start_state, (key_blocks, value_blocks, offsets))
    run_max, run_sum, accumulated = result
    attended = (accumulated / run_sum[..., None]).astype(jnp.bfloat16)
    attended = attended.transpose(0, 3, 1, 2, 4).reshape(
        batch_count, tok_count, kv_local * group_size * HD
    )
    partial_value = jnp.einsum("bte,ed->btd", attended, out_w, preferred_element_type=jnp.float32)
    head_total = lax.psum(partial_value.astype(jnp.bfloat16), "mp").astype(jnp.float32)
    new_hidden = (hidden32 + head_total).astype(jnp.bfloat16)
    return (new_hidden, key_t, value_t)


def per_device(
    series, lengths, patch_weight, norm_gain, query_weight, key_weight, value_weight, out_weight
):
    seq_count, channels, steps_dev = series.shape
    tok_count = steps_dev // STRIDE
    time_count = lax.axis_size("tm")
    time_at = lax.axis_index("tm")
    total_tokens = tok_count * time_count
    tok_start = time_at * tok_count
    step_pos = time_at * steps_dev + jnp.arange(steps_dev, dtype=jnp.int32)
    valid_steps = (step_pos[None, :] >= (steps_dev * time_count - lengths)[:, None]).astype(
        jnp.float32
    )
    masked = series.astype(jnp.float32) * valid_steps[:, None, :]
    history = lengths.astype(jnp.float32)[:, None]
    channel_total = lax.psum(jnp.sum(masked, -1), "tm")
    channel_mean = channel_total / history
    centered = (masked - channel_mean[..., None]) * valid_steps[:, None, :]
    spread_total = lax.psum(jnp.sum(centered * centered, -1), "tm")
    variance = spread_total / history
    normed = (centered * lax.rsqrt(variance + 1e-05)[..., None]).astype(jnp.bfloat16)
    blocks = normed.reshape(seq_count, channels, tok_count, STRIDE)
    column_count = patch_weight.shape[1]
    halves = patch_weight.reshape(channels, 2, STRIDE, column_count)
    right_terms = jnp.einsum(
        "scjr,crd->sjd", blocks, halves[:, 1], preferred_element_type=jnp.float32
    )
    left_all = jnp.einsum("scjr,crd->sjd", blocks, halves[:, 0], preferred_element_type=jnp.float32)
    prior_steps = from_behind(blocks[:, :, tok_count - 1, :], "tm", 1)
    edge_term = jnp.einsum(
        "scr,crd->sd", prior_steps, halves[:, 0], preferred_element_type=jnp.float32
    )
    left_terms = jnp.concatenate([edge_term[:, None, :], left_all[:, : tok_count - 1, :]], 1)
    tokens = (left_terms + right_terms).astype(jnp.bfloat16)
    gathered = lax.all_gather(tokens, ("mp", "section"), axis=2, tiled=True)
    feature_count = gathered.shape[2]
    section_count = lax.axis_size("section")
    section_at = lax.axis_index("section")
    per_section = seq_count // section_count
    head_cols = feature_count // lax.axis_size("mp")
    col_at = lax.axis_index("mp") * head_cols
    kv_local = key_weight.shape[2] // HD
    zero_index = jnp.int32(0)
    key_store = jnp.zeros((1, seq_count, kv_local, HD, tok_count), jnp.bfloat16)
    value_store = jnp.zeros((1, seq_count, kv_local, HD, tok_count), jnp.bfloat16)
    final_store = jnp.zeros((seq_count, tok_count, head_cols), jnp.bfloat16)
    incoming = jnp.zeros((1, tok_count, feature_count), jnp.bfloat16)
    tick_count = seq_count + section_count - 1
    for tick_index in range(tick_count):
        own_rows = gathered[min(tick_index, seq_count - 1)][None]
        current = jnp.where(section_at == 0, own_rows, incoming)
        seq_here = tick_index - section_at
        is_live = (seq_here >= 0) & (seq_here < seq_count)
        seq_slot = jnp.clip(seq_here, 0, seq_count - 1)
        seq_len = lax.dynamic_slice_in_dim(lengths, seq_slot, 1)
        result, key_t, value_t = attend_layer(
            current,
            seq_len,
            norm_gain[0],
            query_weight[0],
            key_weight[0],
            value_weight[0],
            out_weight[0],
            tok_start,
            total_tokens,
        )
        place = (zero_index, seq_slot, zero_index, zero_index, zero_index)
        key_store = jnp.where(
            is_live, lax.dynamic_update_slice(key_store, key_t[None], place), key_store
        )
        value_store = jnp.where(
            is_live, lax.dynamic_update_slice(value_store, value_t[None], place), value_store
        )
        columns = lax.dynamic_slice_in_dim(result, col_at, head_cols, 2)
        is_last = is_live & (section_at == section_count - 1)
        final_store = jnp.where(
            is_last,
            lax.dynamic_update_slice(final_store, columns, (seq_slot, zero_index, zero_index)),
            final_store,
        )
        if tick_index + 1 < tick_count:
            incoming = from_behind(result, "section", 1)
    broadcast_rows = from_root(final_store, "section", section_count - 1)
    final_cols = lax.dynamic_slice_in_dim(broadcast_rows, section_at * per_section, per_section, 0)
    return (key_store, value_store, final_cols)


def solution(mesh):
    in_specs = (
        P("groups", None, "tm"),
        P("groups"),
        P(None, ("mp", "section")),
        P("section", None),
        P("section", None, "mp"),
        P("section", None, "mp"),
        P("section", None, "mp"),
        P("section", "mp", None),
    )
    out_specs = (
        P("section", "groups", "mp", None, "tm"),
        P("section", "groups", "mp", None, "tm"),
        P(("groups", "section"), "tm", "mp"),
    )
    return jax.shard_map(
        per_device, mesh=mesh, in_specs=in_specs, out_specs=out_specs, check_vma=False
    )
```

profile of v0, /device:TPU:0, one launch (start us, length us, event | category | flops | bytes accessed | tf_op | source)
XLA Modules:
  0.0 291.1 jit_solution(578777108349074487)
XLA Ops:
  9.7 13.4 %psum.42 = f32[2,64]{1,0:T(2,128)S(1)} all-reduce(f32[2,64]{1,0:T(2,128)S(1)} %fusion.3), channel_id=1, replica_groups=mesh['groups'=2,'tm'=4,'mp'=2,'section'=2] {'tm'}, use_global_device_ids=true, to_apply=%region_1.0 | all-reduce | flops 128 | bytes 1024 | tf_op jit(solution)/shard_map/psum | solution.py:122
  23.2 1.8 multiply_reduce_fusion
  25.0 8.3 %psum.43 = f32[2,64]{1,0:T(2,128)S(1)} all-reduce(f32[2,64]{1,0:T(2,128)S(1)} %multiply_reduce_fusion), channel_id=1, replica_groups=mesh['groups'=2,'tm'=4,'mp'=2,'section'=2] {'tm'}, use_global_device_ids=true, to_apply=%region_3.0 | all-reduce | flops 128 | bytes 1024 | tf_op jit(solution)/shard_map/psum | solution.py:125
  34.8 5.6 %copy.25 = bf16[2,64,4096]{1,0,2:T(2,128)(2,1)} copy(bf16[2,64,4096]{2,1,0:T(8,128)(2,1)} %multiply_convert_fusion) | data formatting | bytes 2097152 | tf_op jit(solution)/shard_map/convert_element_type | solution.py:127
  41.1 3.9 %collective-permute-start = (bf16[2,64,32]{1,0,2:T(2,128)(2,1)S(1)}, bf16[2,64,32]{1,0,2:T(2,128)(2,1)S(1)}, u32[]{:S(2)}, u32[]{:S(2)}) collective-permute-start(bf16[2,64,32]{1,0,2:T(2,128)(2,1)S(1)} %slice_bitcast_fusion), channel_id=1, source_target_pairs={{0,4},{4,8},{8,12},{1,5},{5,9},{9,13},{2,6},{6,10},{10,14},{3,7},{... | collective-permute-start | bytes 24584 | tf_op jit(solution)/shard_map/ppermute | solution.py:13
  53.4 5.5 %copy.28 = bf16[2,64,128,32]{2,1,3,0:T(8,128)(2,1)} copy(bf16[2,64,128,32]{1,0,3,2:T(2,128)(2,1)} %bitcast.265) | data formatting | bytes 2097152 | tf_op jit(solution)/shard_map/reshape | solution.py:128
  58.9 4.5 %copy.26 = bf16[4096,320]{1,0:T(8,128)(2,1)} copy(bf16[4096,320]{0,1:T(8,128)(2,1)} %param.10) | data formatting | bytes 5242880 | tf_op args[2]
  63.4 2.3 fusion.128
  69.4 2.0 fusion.59
  72.4 2.2 fusion.46
  74.6 8.0 %all_gather.21 = bf16[2,128,1280]{1,2,0:T(8,128)(2,1)S(1)} all-gather(bf16[2,128,320]{1,2,0:T(8,128)(2,1)S(1)} %fusion.46), channel_id=1, replica_groups=mesh['groups'=2,'tm'=4,'mp'=2,'section'=2] {'mp','section'}, dimensions={2}, use_global_device_ids=true | all-gather | bytes 819200 | tf_op jit(solution)/shard_map/all_gather | solution.py:141
  85.0 13.2 %all_gather.23 = bf16[1,2,80,512]{3,2,1,0:T(8,128)(2,1)} all-gather(bf16[1,2,80,128]{3,2,1,0:T(8,128)(2,1)S(1)} %bitcast.283), channel_id=1, replica_groups=mesh['groups'=2,'tm'=4,'mp'=2,'section'=2] {'tm'}, dimensions={3}, use_global_device_ids=true | all-gather | bytes 204800 | tf_op jit(solution)/shard_map/all_gather | solution.py:76
  98.2 12.4 %all_gather.22 = bf16[1,2,80,512]{3,2,1,0:T(8,128)(2,1)S(1)} all-gather(bf16[1,2,80,128]{3,2,1,0:T(8,128)(2,1)S(1)} %bitcast.282), channel_id=1, replica_groups=mesh['groups'=2,'tm'=4,'mp'=2,'section'=2] {'tm'}, dimensions={3}, use_global_device_ids=true | all-gather | bytes 204800 | tf_op jit(solution)/shard_map/all_gather | solution.py:75
  117.6 22.0 %all-reduce.5.cloned.1.call-done = bf16[1,128,1280]{1,2,0:T(8,128)(2,1)} async-done(((bf16[1,128,1280]{1,2,0:T(8,128)(2,1)}), bf16[1,128,1280]{1,2,0:T(8,128)(2,1)}) %all-reduce.5.cloned.1.call-update) | async-done | bytes 327696 | tf_op jit(solution)/shard_map/psum | solution.py:102
  140.8 1.7 collective-permute-start.1
  148.3 12.4 %all_gather.24 = bf16[1,2,80,512]{3,2,1,0:T(8,128)(2,1)S(1)} all-gather(bf16[1,2,80,128]{3,2,1,0:T(8,128)(2,1)S(1)} %bitcast.274), channel_id=1, replica_groups=mesh['groups'=2,'tm'=4,'mp'=2,'section'=2] {'tm'}, dimensions={3}, use_global_device_ids=true | all-gather | bytes 204800 | tf_op jit(solution)/shard_map/all_gather | solution.py:75
  162.5 12.7 %all_gather.25 = bf16[1,2,80,512]{3,2,1,0:T(8,128)(2,1)S(1)} all-gather(bf16[1,2,80,128]{3,2,1,0:T(8,128)(2,1)S(1)} %bitcast.272), channel_id=1, replica_groups=mesh['groups'=2,'tm'=4,'mp'=2,'section'=2] {'tm'}, dimensions={3}, use_global_device_ids=true | all-gather | bytes 204800 | tf_op jit(solution)/shard_map/all_gather | solution.py:76
  180.7 20.6 %all-reduce.7.cloned.1.call-done = bf16[1,128,1280]{1,2,0:T(8,128)(2,1)} async-done(((bf16[1,128,1280]{1,2,0:T(8,128)(2,1)}), bf16[1,128,1280]{1,2,0:T(8,128)(2,1)}) %all-reduce.7.cloned.1.call-update) | async-done | bytes 327696 | tf_op jit(solution)/shard_map/psum | solution.py:102
  202.6 1.9 collective-permute-start.2
  206.4 1.9 fusion.127
  211.5 12.6 %all_gather.27 = bf16[1,2,80,512]{3,2,1,0:T(8,128)(2,1)S(1)} all-gather(bf16[1,2,80,128]{3,2,1,0:T(8,128)(2,1)} %bitcast.276), channel_id=1, replica_groups=mesh['groups'=2,'tm'=4,'mp'=2,'section'=2] {'tm'}, dimensions={3}, use_global_device_ids=true | all-gather | bytes 204800 | tf_op jit(solution)/shard_map/all_gather | solution.py:76
  224.1 12.6 %all_gather.26 = bf16[1,2,80,512]{3,2,1,0:T(8,128)(2,1)S(1)} all-gather(bf16[1,2,80,128]{3,2,1,0:T(8,128)(2,1)} %bitcast.278), channel_id=1, replica_groups=mesh['groups'=2,'tm'=4,'mp'=2,'section'=2] {'tm'}, dimensions={3}, use_global_device_ids=true | all-gather | bytes 204800 | tf_op jit(solution)/shard_map/all_gather | solution.py:75
  239.9 22.2 %all-reduce.9.cloned.1.call-done = bf16[1,128,1280]{1,2,0:T(8,128)(2,1)} async-done(((bf16[1,128,1280]{1,2,0:T(8,128)(2,1)}), bf16[1,128,1280]{1,2,0:T(8,128)(2,1)}) %all-reduce.9.cloned.1.call-update) | async-done | bytes 327696 | tf_op jit(solution)/shard_map/psum | solution.py:102
  264.0 18.8 %all-reduce.11.cloned.1.call-done = bf16[2,128,640]{1,2,0:T(8,128)(2,1)} async-done(((bf16[2,128,640]{1,2,0:T(8,128)(2,1)}), bf16[2,128,640]{1,2,0:T(8,128)(2,1)}) %all-reduce.11.cloned.1.call-update) | async-done | bytes 327696 | tf_op jit(solution)/shard_map/psum | solution.py:18
  (144 shorter events, 46.4 us)
Async XLA Ops:
  7.2 108.9 %copy-start = (bf16[1,640,1280]{2,1,0:T(8,128)(2,1)S(1)}, bf16[1,640,1280]{2,1,0:T(8,128)(2,1)}, u32[]{:S(2)}) copy-start(bf16[1,640,1280]{2,1,0:T(8,128)(2,1)} %param.15) | copy-start | bytes 4915204
  7.2 26.2 %copy-start.1 = (bf16[2,64,4096]{2,1,0:T(8,128)(2,1)S(1)}, bf16[2,64,4096]{2,1,0:T(8,128)(2,1)}, u32[]{:S(2)}) copy-start(bf16[2,64,4096]{2,1,0:T(8,128)(2,1)} %param.8) | copy-start | bytes 3145732
  7.2 132.4 %all-reduce.5.cloned.1.call-start = ((), (), s32[]{:S(2)}) async-start(), calls=%async_computation | async-start | bytes 655360 | tf_op jit(solution)/shard_map/psum | solution.py:102
  34.8 10.2 %copy-start.26 = (s32[2]{0:T(128)S(1)}, s32[2]{0:T(128)}, u32[]{:S(2)}) copy-start(s32[2]{0:T(128)} %param.9) | copy-start | bytes 28
  41.1 28.3 %collective-permute-start = (bf16[2,64,32]{1,0,2:T(2,128)(2,1)S(1)}, bf16[2,64,32]{1,0,2:T(2,128)(2,1)S(1)}, u32[]{:S(2)}, u32[]{:S(2)}) collective-permute-start(bf16[2,64,32]{1,0,2:T(2,128)(2,1)S(1)} %slice_bitcast_fusion), channel_id=1, source_target_pairs={{0,4},{4,8},{8,12},{1,5},{5,9},{9,13},{2,6},{6,10},{10,14},{3,7},{... | collective-permute-start | bytes 24584 | tf_op jit(solution)/shard_map/ppermute | solution.py:13
  72.4 10.5 %copy-start.27 = (bf16[1,1280,160]{1,2,0:T(8,128)(2,1)S(1)}, bf16[1,1280,160]{1,2,0:T(8,128)(2,1)}, u32[]{:S(2)}) copy-start(bf16[1,1280,160]{1,2,0:T(8,128)(2,1)} %param.13) | copy-start | bytes 1228804
  74.6 9.3 %copy-start.29 = (bf16[1,1280,160]{1,2,0:T(8,128)(2,1)S(1)}, bf16[1,1280,160]{1,2,0:T(8,128)(2,1)}, u32[]{:S(2)}) copy-start(bf16[1,1280,160]{1,2,0:T(8,128)(2,1)} %param.14) | copy-start | bytes 1228804
  74.6 35.9 %copy-start.2 = (bf16[1,1280,640]{2,1,0:T(8,128)(2,1)S(1)}, bf16[1,1280,640]{2,1,0:T(8,128)(2,1)}, u32[]{:S(2)}) copy-start(bf16[1,1280,640]{2,1,0:T(8,128)(2,1)} %param.12) | copy-start | bytes 4915204
  82.7 27.9 %copy-start.3 = (bf16[2,128,1280]{1,2,0:T(8,128)(2,1)}, bf16[2,128,1280]{1,2,0:T(8,128)(2,1)S(1)}, u32[]{:S(2)}) copy-start(bf16[2,128,1280]{1,2,0:T(8,128)(2,1)S(1)} %all_gather.21) | copy-start | bytes 1966084
  117.6 83.8 %all-reduce.7.cloned.1.call-start = ((), (), s32[]{:S(2)}) async-start(), calls=%async_computation.1 | async-start | bytes 655360 | tf_op jit(solution)/shard_map/psum | solution.py:102
  140.8 3.0 %collective-permute-start.1 = (bf16[1,128,1280]{1,2,0:T(8,128)(2,1)S(1)}, bf16[1,128,1280]{1,2,0:T(8,128)(2,1)S(1)}, u32[]{:S(2)}, u32[]{:S(2)}) collective-permute-start(bf16[1,128,1280]{1,2,0:T(8,128)(2,1)S(1)} %fusion.80), channel_id=1, source_target_pairs={{0,1},{2,3},{4,5},{6,7},{8,9},{10,11},{12,13},{14,15},{16,17},{18,... | collective-permute-start | bytes 983048 | tf_op jit(solution)/shard_map/ppermute | solution.py:13
  162.5 14.1 %copy-start.13 = (pred[128,512]{0,1:T(8,128)(4,1)S(1)}, pred[128,512]{0,1:T(8,128)(4,1)}, u32[]{:S(2)}) copy-start(pred[128,512]{0,1:T(8,128)(4,1)} %get-tuple-element.94) | copy-start | bytes 196612
  179.0 83.1 %all-reduce.9.cloned.1.call-start = ((), (), s32[]{:S(2)}) async-start(), calls=%async_computation.2 | async-start | bytes 655360 | tf_op jit(solution)/shard_map/psum | solution.py:102
  180.7 28.8 %copy-start.18 = (bf16[1,2,2,80,128]{4,3,2,1,0:T(8,128)(2,1)}, bf16[1,2,2,80,128]{4,3,2,1,0:T(8,128)(2,1)S(1)}, u32[]{:S(2)}) copy-start(bf16[1,2,2,80,128]{4,3,2,1,0:T(8,128)(2,1)S(1)} %constant_dynamic-update-slice_fusion) | copy-start | bytes 245764
  201.3 7.2 %copy-start.28 = (bf16[1,1280,160]{1,2,0:T(8,128)(2,1)S(1)}, bf16[1,1280,160]{1,2,0:T(8,128)(2,1)}, u32[]{:S(2)}) copy-start(bf16[1,1280,160]{1,2,0:T(8,128)(2,1)} %param.13) | copy-start | bytes 1228804
  202.6 7.0 %copy-start.31 = (bf16[1,1280,160]{1,2,0:T(8,128)(2,1)S(1)}, bf16[1,1280,160]{1,2,0:T(8,128)(2,1)}, u32[]{:S(2)}) copy-start(bf16[1,1280,160]{1,2,0:T(8,128)(2,1)} %param.14) | copy-start | bytes 1228804
  202.6 3.8 %collective-permute-start.2 = (bf16[1,128,1280]{1,2,0:T(8,128)(2,1)S(1)}, bf16[1,128,1280]{1,2,0:T(8,128)(2,1)S(1)}, u32[]{:S(2)}, u32[]{:S(2)}) collective-permute-start(bf16[1,128,1280]{1,2,0:T(8,128)(2,1)S(1)} %fusion.84), channel_id=1, source_target_pairs={{0,1},{2,3},{4,5},{6,7},{8,9},{10,11},{12,13},{14,15},{16,17},{18,... | collective-permute-start | bytes 983048 | tf_op jit(solution)/shard_map/ppermute | solution.py:13
  238.2 23.9 %copy-start.8 = (f32[1,128,1280]{1,2,0:T(8,128)S(1)}, f32[1,128,1280]{1,2,0:T(8,128)}, u32[]{:S(2)}) copy-start(f32[1,128,1280]{1,2,0:T(8,128)} %get-tuple-element.72) | copy-start | bytes 1966084
  238.2 25.7 %copy-start.16 = (bf16[1,2,2,80,128]{4,3,2,1,0:T(8,128)(2,1)S(1)}, bf16[1,2,2,80,128]{4,3,2,1,0:T(8,128)(2,1)}, u32[]{:S(2)}) copy-start(bf16[1,2,2,80,128]{4,3,2,1,0:T(8,128)(2,1)} %copy-done.15) | copy-start | bytes 245764
  238.2 25.7 %copy-start.24 = (bf16[128,160]{0,1:T(8,128)(2,1)S(1)}, bf16[128,160]{0,1:T(8,128)(2,1)}, u32[]{:S(2)}) copy-start(bf16[128,160]{0,1:T(8,128)(2,1)} %convolution_convert_fusion.4) | copy-start | bytes 122884
  238.2 25.7 %copy-start.23 = (bf16[128,160]{0,1:T(8,128)(2,1)S(1)}, bf16[128,160]{0,1:T(8,128)(2,1)}, u32[]{:S(2)}) copy-start(bf16[128,160]{0,1:T(8,128)(2,1)} %convolution_convert_fusion.3) | copy-start | bytes 122884
  239.7 43.1 %all-reduce.11.cloned.1.call-start = ((), (), s32[]{:S(2)}) async-start(), calls=%async_computation.3 | async-start | bytes 655360 | tf_op jit(solution)/shard_map/psum | solution.py:18
  263.9 20.6 %copy-start.17 = (bf16[1,2,2,80,128]{4,3,2,1,0:T(8,128)(2,1)}, bf16[1,2,2,80,128]{4,3,2,1,0:T(8,128)(2,1)S(1)}, u32[]{:S(2)}) copy-start(bf16[1,2,2,80,128]{4,3,2,1,0:T(8,128)(2,1)S(1)} %select_dynamic-update-slice_fusion.4) | copy-start | bytes 245764
  264.0 20.6 %copy-start.20 = (bf16[1,2,2,80,128]{4,3,2,1,0:T(8,128)(2,1)}, bf16[1,2,2,80,128]{4,3,2,1,0:T(8,128)(2,1)S(1)}, u32[]{:S(2)}) copy-start(bf16[1,2,2,80,128]{4,3,2,1,0:T(8,128)(2,1)S(1)} %select_dynamic-update-slice_fusion.2) | copy-start | bytes 245764
  (15 other events, 36.9 us)
Sparse Core Ops, SparseCore 0:
  117.7 21.8 all-reduce.4
  179.2 22.1 all-reduce.6
  239.8 22.2 all-reduce.8
  264.4 18.3 all-reduce.10
where the time goes:
time: 293 us; the launch traced here: 291 us
  blocking collectives  106 us (36%)
  waiting for transfers between devices  84.9 us (29%)
  local copies, waits for them, and re-layouts  28.5 us (10%)
  matrix products  24.7 us (8%)
  between operations  22.1 us (8%)
  other arithmetic  17.6 us (6%)
  starting transfers between devices  7.62 us (3%)
    psum x3, waiting for transfers between devices, attend_layer(): lax.psum(partial_value.astype(jnp.bfloat16), 'mp').astype(jnp.float32)  64.8 us
    all_gather x3, blocking collectives, attend_layer(): value_piece = lax.all_gather(value_t, 'tm', axis=3, tiled=True)  38.5 us
    all_gather x3, blocking collectives, attend_layer(): key_piece = lax.all_gather(key_t, 'tm', axis=3, tiled=True)  37.4 us
    psum x1, waiting for transfers between devices, from_root(): return lax.psum(jnp.where(mine, value, jnp.zeros_like(value)), axis)  18.8 us
    psum x1, blocking collectives, per_device(): channel_total = lax.psum(jnp.sum(masked, -1), 'tm')  13.4 us
    psum x1, blocking collectives, per_device(): spread_total = lax.psum(jnp.sum(centered * centered, -1), 'tm')  8.34 us
    all_gather x1, blocking collectives, per_device(): gathered = lax.all_gather(tokens, ('mp', 'section'), axis=2, tiled=True)  8.02 us
    ppermute x3, starting transfers between devices, from_behind(): return lax.ppermute(value, axis, pairs)  7.46 us
  transfers between devices with their start and end apart: 7, of which 5 were waited for; matrix products, arithmetic and copies ran while one was open for 7% of the time, Pallas kernels for 0%

commit v1 on v0

--- a/solution.py
+++ b/solution.py
@@ -5,6 +5,12 @@
 
 STRIDE = 32
 HD = 80
+
+
+def gather_and_add(block, name):
+    terms = lax.all_gather(block, name, axis=0, tiled=False)
+    summed = terms.sum(axis=0)
+    return summed
 
 
 def from_behind(value, axis, by):
@@ -99,7 +105,7 @@
         batch_count, tok_count, kv_local * group_size * HD
     )
     partial_value = jnp.einsum("bte,ed->btd", attended, out_w, preferred_element_type=jnp.float32)
-    head_total = lax.psum(partial_value.astype(jnp.bfloat16), "mp").astype(jnp.float32)
+    head_total = gather_and_add(partial_value.astype(jnp.bfloat16), "mp").astype(jnp.float32)
     new_hidden = (hidden32 + head_total).astype(jnp.bfloat16)
     return (new_hidden, key_t, value_t)
 

time: 293 us -> 250 us (0.85)
  waiting for transfers between devices: 84.9 us -> 16.3 us
  blocking collectives: 106 us -> 130 us
  matrix products: 24.7 us -> 19.3 us
  local copies, waits for them, and re-layouts: 28.5 us -> 32.6 us
  other arithmetic: 17.6 us -> 21.3 us
    psum x3 -> x0, waiting for transfers between devices: 64.8 us -> none  [attend_layer(): lax.psum(partial_value.astype(jnp.bfloat16), 'mp').astype(jnp.float32)]
    all_gather x0 -> x3, blocking collectives: none -> 23.7 us  [gather_and_add(): terms = lax.all_gather(block, name, axis=0, tiled=False)]
    reduce_sum x0 -> x3, local copies, waits for them, and re-layouts: none -> 4.95 us  [gather_and_add(): summed = terms.sum(axis=0)]
    reduce_sum x0 -> x3, other arithmetic: none -> 4.93 us  [gather_and_add(): summed = terms.sum(axis=0)]
    dot_general x3, matrix products: 4.4 us -> 1.36 us  [attend_layer(): jnp.einsum('bte,ed->btd', attended, out_w, preferred_element_type=jnp.flo...]
    unnamed x66 -> x72, local copies, waits for them, and re-layouts: 6.62 us -> 7.4 us
  transfers between devices with their start and end apart: 7 -> 4, of which waited for: 5 -> 2; matrix products, arithmetic and copies ran while one was open for 7% -> 7% of each run, Pallas kernels for 0% -> 0%
where the time goes in v1:
time: 250 us; the launch traced here: 248 us
  blocking collectives  130 us (52%)
  local copies, waits for them, and re-layouts  32.6 us (13%)
  between operations  22.4 us (9%)
  other arithmetic  21.3 us (9%)
  matrix products  19.3 us (8%)
  waiting for transfers between devices  16.3 us (7%)
  starting transfers between devices  6.53 us (3%)
    all_gather x3, blocking collectives, attend_layer(): value_piece = lax.all_gather(value_t, 'tm', axis=3, tiled=True)  38.3 us
    all_gather x3, blocking collectives, attend_layer(): key_piece = lax.all_gather(key_t, 'tm', axis=3, tiled=True)  37.8 us
    all_gather x3, blocking collectives, gather_and_add(): terms = lax.all_gather(block, name, axis=0, tiled=False)  23.7 us
    psum x1, waiting for transfers between devices, from_root(): return lax.psum(jnp.where(mine, value, jnp.zeros_like(value)), axis)  16 us
    psum x1, blocking collectives, per_device(): channel_total = lax.psum(jnp.sum(masked, -1), 'tm')  13.4 us
    psum x1, blocking collectives, per_device(): spread_total = lax.psum(jnp.sum(centered * centered, -1), 'tm')  8.34 us
    all_gather x1, blocking collectives, per_device(): gathered = lax.all_gather(tokens, ('mp', 'section'), axis=2, tiled=True)  8.02 us
    unnamed x72, local copies, waits for them, and re-layouts  7.4 us
  transfers between devices with their start and end apart: 4, of which 2 were waited for; matrix products, arithmetic and copies ran while one was open for 7% of the time, Pallas kernels for 0%

profile of v1, /device:TPU:0, one launch (start us, length us, event | category | flops | bytes accessed | tf_op | source)
XLA Modules:
  0.0 248.1 jit_solution(220440323562897756)
XLA Ops:
  9.7 13.4 %psum.21 = f32[2,64]{1,0:T(2,128)S(1)} all-reduce(f32[2,64]{1,0:T(2,128)S(1)} %fusion), channel_id=1, replica_groups=mesh['groups'=2,'tm'=4,'mp'=2,'section'=2] {'tm'}, use_global_device_ids=true, to_apply=%region_1.0 | all-reduce | flops 128 | bytes 1024 | tf_op jit(solution)/shard_map/psum | solution.py:128
  25.0 8.3 %psum.22 = f32[2,64]{1,0:T(2,128)S(1)} all-reduce(f32[2,64]{1,0:T(2,128)S(1)} %multiply_reduce_fusion), channel_id=1, replica_groups=mesh['groups'=2,'tm'=4,'mp'=2,'section'=2] {'tm'}, use_global_device_ids=true, to_apply=%region_3.0 | all-reduce | flops 128 | bytes 1024 | tf_op jit(solution)/shard_map/psum | solution.py:131
  34.8 5.5 %copy.36 = bf16[2,64,4096]{1,0,2:T(2,128)(2,1)} copy(bf16[2,64,4096]{2,1,0:T(8,128)(2,1)} %multiply_convert_fusion) | data formatting | bytes 2097152 | tf_op jit(solution)/shard_map/convert_element_type | solution.py:133
  41.1 3.9 %collective-permute-start = (bf16[2,64,32]{1,0,2:T(2,128)(2,1)S(1)}, bf16[2,64,32]{1,0,2:T(2,128)(2,1)S(1)}, u32[]{:S(2)}, u32[]{:S(2)}) collective-permute-start(bf16[2,64,32]{1,0,2:T(2,128)(2,1)S(1)} %slice_bitcast_fusion), channel_id=1, source_target_pairs={{0,4},{4,8},{8,12},{1,5},{5,9},{9,13},{2,6},{6,10},{10,14},{3,7},{... | collective-permute-start | bytes 24584 | tf_op jit(solution)/shard_map/ppermute | solution.py:19
  53.4 5.5 %copy.39 = bf16[2,64,128,32]{2,1,3,0:T(8,128)(2,1)} copy(bf16[2,64,128,32]{1,0,3,2:T(2,128)(2,1)} %bitcast.270) | data formatting | bytes 2097152 | tf_op jit(solution)/shard_map/reshape | solution.py:134
  58.9 4.6 %copy.37 = bf16[4096,320]{1,0:T(8,128)(2,1)} copy(bf16[4096,320]{0,1:T(8,128)(2,1)} %param.10) | data formatting | bytes 5242880 | tf_op args[2]
  63.5 2.3 fusion.125
  69.5 2.0 fusion.56
  72.4 2.2 fusion.43
  74.7 8.0 %all_gather.39 = bf16[2,128,1280]{1,2,0:T(8,128)(2,1)S(1)} all-gather(bf16[2,128,320]{1,2,0:T(8,128)(2,1)S(1)} %fusion.43), channel_id=1, replica_groups=mesh['groups'=2,'tm'=4,'mp'=2,'section'=2] {'mp','section'}, dimensions={2}, use_global_device_ids=true | all-gather | bytes 819200 | tf_op jit(solution)/shard_map/all_gather | solution.py:147
  84.4 13.2 %all_gather.41 = bf16[1,2,80,512]{3,2,1,0:T(8,128)(2,1)} all-gather(bf16[1,2,80,128]{3,2,1,0:T(8,128)(2,1)S(1)} %bitcast.292), channel_id=1, replica_groups=mesh['groups'=2,'tm'=4,'mp'=2,'section'=2] {'tm'}, dimensions={3}, use_global_device_ids=true | all-gather | bytes 204800 | tf_op jit(solution)/shard_map/all_gather | solution.py:82
  97.6 12.4 %all_gather.40 = bf16[1,2,80,512]{3,2,1,0:T(8,128)(2,1)S(1)} all-gather(bf16[1,2,80,128]{3,2,1,0:T(8,128)(2,1)S(1)} %bitcast.291), channel_id=1, replica_groups=mesh['groups'=2,'tm'=4,'mp'=2,'section'=2] {'tm'}, dimensions={3}, use_global_device_ids=true | all-gather | bytes 204800 | tf_op jit(solution)/shard_map/all_gather | solution.py:81
  116.0 7.9 %all-gather = bf16[256,1280]{1,0:T(8,128)(2,1)} all-gather(bf16[128,1280]{1,0:T(8,128)(2,1)S(1)} %convolution_convert_fusion.2), channel_id=2, replica_groups=mesh['groups'=2,'tm'=4,'mp'=2,'section'=2] {'mp'}, dimensions={0}, use_global_device_ids=true | all-gather | bytes 983040 | tf_op jit(solution)/shard_map/all_gather | solution.py:11
  123.8 2.0 reduce.15
  125.8 1.9 copy.45
  134.0 12.7 %all_gather.44 = bf16[1,2,80,512]{3,2,1,0:T(8,128)(2,1)S(1)} all-gather(bf16[1,2,80,128]{3,2,1,0:T(8,128)(2,1)S(1)} %bitcast.287), channel_id=1, replica_groups=mesh['groups'=2,'tm'=4,'mp'=2,'section'=2] {'tm'}, dimensions={3}, use_global_device_ids=true | all-gather | bytes 204800 | tf_op jit(solution)/shard_map/all_gather | solution.py:81
  148.4 12.7 %all_gather.45 = bf16[1,2,80,512]{3,2,1,0:T(8,128)(2,1)S(1)} all-gather(bf16[1,2,80,128]{3,2,1,0:T(8,128)(2,1)S(1)} %bitcast.285), channel_id=1, replica_groups=mesh['groups'=2,'tm'=4,'mp'=2,'section'=2] {'tm'}, dimensions={3}, use_global_device_ids=true | all-gather | bytes 204800 | tf_op jit(solution)/shard_map/all_gather | solution.py:82
  164.0 8.0 %all-gather.1 = bf16[256,1280]{1,0:T(8,128)(2,1)} all-gather(bf16[128,1280]{1,0:T(8,128)(2,1)S(1)} %convolution_convert_fusion.1), channel_id=3, replica_groups=mesh['groups'=2,'tm'=4,'mp'=2,'section'=2] {'mp'}, dimensions={0}, use_global_device_ids=true | all-gather | bytes 983040 | tf_op jit(solution)/shard_map/all_gather | solution.py:11
  172.0 2.0 reduce.16
  181.0 1.9 fusion.124
  185.4 12.4 %all_gather.49 = bf16[1,2,80,512]{3,2,1,0:T(8,128)(2,1)S(1)} all-gather(bf16[1,2,80,128]{3,2,1,0:T(8,128)(2,1)S(1)} %bitcast.281), channel_id=1, replica_groups=mesh['groups'=2,'tm'=4,'mp'=2,'section'=2] {'tm'}, dimensions={3}, use_global_device_ids=true | all-gather | bytes 204800 | tf_op jit(solution)/shard_map/all_gather | solution.py:82
  197.8 12.7 %all_gather.48 = bf16[1,2,80,512]{3,2,1,0:T(8,128)(2,1)S(1)} all-gather(bf16[1,2,80,128]{3,2,1,0:T(8,128)(2,1)} %bitcast.283), channel_id=1, replica_groups=mesh['groups'=2,'tm'=4,'mp'=2,'section'=2] {'tm'}, dimensions={3}, use_global_device_ids=true | all-gather | bytes 204800 | tf_op jit(solution)/shard_map/all_gather | solution.py:81
  212.5 7.9 %all-gather.2 = bf16[256,1280]{1,0:T(8,128)(2,1)S(1)} all-gather(bf16[128,1280]{1,0:T(8,128)(2,1)S(1)} %convolution_convert_fusion), channel_id=4, replica_groups=mesh['groups'=2,'tm'=4,'mp'=2,'section'=2] {'mp'}, dimensions={0}, use_global_device_ids=true | all-gather | bytes 983040 | tf_op jit(solution)/shard_map/all_gather | solution.py:11
  223.5 16.0 %all-reduce.2.cloned.1.call-done = bf16[2,128,640]{1,2,0:T(8,128)(2,1)} async-done(((bf16[2,128,640]{1,2,0:T(8,128)(2,1)}), bf16[2,128,640]{1,2,0:T(8,128)(2,1)}) %all-reduce.2.cloned.1.call-update) | async-done | bytes 327696 | tf_op jit(solution)/shard_map/psum | solution.py:24
  (150 shorter events, 46.2 us)
Async XLA Ops:
  7.2 108.3 %copy-start = (bf16[1,640,1280]{2,1,0:T(8,128)(2,1)S(1)}, bf16[1,640,1280]{2,1,0:T(8,128)(2,1)}, u32[]{:S(2)}) copy-start(bf16[1,640,1280]{2,1,0:T(8,128)(2,1)} %param.15) | copy-start | bytes 4915204
  7.2 26.2 %copy-start.1 = (bf16[2,64,4096]{2,1,0:T(8,128)(2,1)S(1)}, bf16[2,64,4096]{2,1,0:T(8,128)(2,1)}, u32[]{:S(2)}) copy-start(bf16[2,64,4096]{2,1,0:T(8,128)(2,1)} %param.8) | copy-start | bytes 3145732
  7.2 232.3 %all-reduce.2.cloned.1.call-start = ((), (), s32[]{:S(2)}) async-start(), calls=%async_computation | async-start | bytes 655360 | tf_op jit(solution)/shard_map/psum | solution.py:24
  34.8 10.2 %copy-start.28 = (s32[2]{0:T(128)S(1)}, s32[2]{0:T(128)}, u32[]{:S(2)}) copy-start(s32[2]{0:T(128)} %param.9) | copy-start | bytes 28
  41.1 28.4 %collective-permute-start = (bf16[2,64,32]{1,0,2:T(2,128)(2,1)S(1)}, bf16[2,64,32]{1,0,2:T(2,128)(2,1)S(1)}, u32[]{:S(2)}, u32[]{:S(2)}) collective-permute-start(bf16[2,64,32]{1,0,2:T(2,128)(2,1)S(1)} %slice_bitcast_fusion), channel_id=1, source_target_pairs={{0,4},{4,8},{8,12},{1,5},{5,9},{9,13},{2,6},{6,10},{10,14},{3,7},{... | collective-permute-start | bytes 24584 | tf_op jit(solution)/shard_map/ppermute | solution.py:19
  72.4 10.5 %copy-start.29 = (bf16[1,1280,160]{1,2,0:T(8,128)(2,1)S(1)}, bf16[1,1280,160]{1,2,0:T(8,128)(2,1)}, u32[]{:S(2)}) copy-start(bf16[1,1280,160]{1,2,0:T(8,128)(2,1)} %param.13) | copy-start | bytes 1228804
  74.6 9.3 %copy-start.32 = (bf16[1,1280,160]{1,2,0:T(8,128)(2,1)S(1)}, bf16[1,1280,160]{1,2,0:T(8,128)(2,1)}, u32[]{:S(2)}) copy-start(bf16[1,1280,160]{1,2,0:T(8,128)(2,1)} %param.14) | copy-start | bytes 1228804
  74.7 35.3 %copy-start.2 = (bf16[1,1280,640]{2,1,0:T(8,128)(2,1)S(1)}, bf16[1,1280,640]{2,1,0:T(8,128)(2,1)}, u32[]{:S(2)}) copy-start(bf16[1,1280,640]{2,1,0:T(8,128)(2,1)} %param.12) | copy-start | bytes 4915204
  82.7 27.3 %copy-start.3 = (bf16[2,128,1280]{1,2,0:T(8,128)(2,1)}, bf16[2,128,1280]{1,2,0:T(8,128)(2,1)S(1)}, u32[]{:S(2)}) copy-start(bf16[2,128,1280]{1,2,0:T(8,128)(2,1)S(1)} %all_gather.39) | copy-start | bytes 1966084
  115.9 14.4 %copy-start.26 = (bf16[160,128]{1,0:T(8,128)(2,1)S(1)}, bf16[160,128]{1,0:T(8,128)(2,1)}, u32[]{:S(2)}) copy-start(bf16[160,128]{1,0:T(8,128)(2,1)} %get-tuple-element.113) | copy-start | bytes 122884
  129.0 2.5 %collective-permute-start.1 = (bf16[1,128,1280]{1,2,0:T(8,128)(2,1)S(1)}, bf16[1,128,1280]{1,2,0:T(8,128)(2,1)S(1)}, u32[]{:S(2)}, u32[]{:S(2)}) collective-permute-start(bf16[1,128,1280]{1,2,0:T(8,128)(2,1)S(1)} %fusion.77), channel_id=1, source_target_pairs={{0,1},{2,3},{4,5},{6,7},{8,9},{10,11},{12,13},{14,15},{16,17},{18,... | collective-permute-start | bytes 983048 | tf_op jit(solution)/shard_map/ppermute | solution.py:19
  148.4 14.1 %copy-start.11 = (pred[128,512]{0,1:T(8,128)(4,1)S(1)}, pred[128,512]{0,1:T(8,128)(4,1)}, u32[]{:S(2)}) copy-start(pred[128,512]{0,1:T(8,128)(4,1)} %get-tuple-element.97) | copy-start | bytes 196612
  164.0 14.5 %copy-start.14 = (bf16[1,2,2,80,128]{4,3,2,1,0:T(8,128)(2,1)S(1)}, bf16[1,2,2,80,128]{4,3,2,1,0:T(8,128)(2,1)}, u32[]{:S(2)}) copy-start(bf16[1,2,2,80,128]{4,3,2,1,0:T(8,128)(2,1)} %copy-done.13) | copy-start | bytes 245764
  164.0 17.0 %copy-start.19 = (bf16[1,2,2,80,128]{4,3,2,1,0:T(8,128)(2,1)S(1)}, bf16[1,2,2,80,128]{4,3,2,1,0:T(8,128)(2,1)}, u32[]{:S(2)}) copy-start(bf16[1,2,2,80,128]{4,3,2,1,0:T(8,128)(2,1)} %copy-done.18) | copy-start | bytes 245764
  175.9 7.2 %copy-start.31 = (bf16[1,1280,160]{1,2,0:T(8,128)(2,1)S(1)}, bf16[1,1280,160]{1,2,0:T(8,128)(2,1)}, u32[]{:S(2)}) copy-start(bf16[1,1280,160]{1,2,0:T(8,128)(2,1)} %param.13) | copy-start | bytes 1228804
  175.9 8.3 %copy-start.34 = (bf16[1,1280,160]{1,2,0:T(8,128)(2,1)S(1)}, bf16[1,1280,160]{1,2,0:T(8,128)(2,1)}, u32[]{:S(2)}) copy-start(bf16[1,1280,160]{1,2,0:T(8,128)(2,1)} %param.14) | copy-start | bytes 1228804
  177.1 3.8 %collective-permute-start.2 = (bf16[1,128,1280]{1,2,0:T(8,128)(2,1)S(1)}, bf16[1,128,1280]{1,2,0:T(8,128)(2,1)S(1)}, u32[]{:S(2)}, u32[]{:S(2)}) collective-permute-start(bf16[1,128,1280]{1,2,0:T(8,128)(2,1)S(1)} %fusion.81), channel_id=1, source_target_pairs={{0,1},{2,3},{4,5},{6,7},{8,9},{10,11},{12,13},{14,15},{16,17},{18,... | collective-permute-start | bytes 983048 | tf_op jit(solution)/shard_map/ppermute | solution.py:19
  212.0 10.5 %copy-start.7 = (bf16[2,128,640]{1,2,0:T(8,128)(2,1)S(1)}, bf16[2,128,640]{1,2,0:T(8,128)(2,1)}, u32[]{:S(2)}) copy-start(bf16[2,128,640]{1,2,0:T(8,128)(2,1)} %select_dynamic-update-slice_fusion) | copy-start | bytes 983044
  212.0 10.5 %copy-start.9 = (f32[1,128,1280]{1,2,0:T(8,128)S(1)}, f32[1,128,1280]{1,2,0:T(8,128)}, u32[]{:S(2)}) copy-start(f32[1,128,1280]{1,2,0:T(8,128)} %get-tuple-element.75) | copy-start | bytes 1966084
  212.5 10.9 %copy-start.16 = (bf16[1,2,2,80,128]{4,3,2,1,0:T(8,128)(2,1)S(1)}, bf16[1,2,2,80,128]{4,3,2,1,0:T(8,128)(2,1)}, u32[]{:S(2)}) copy-start(bf16[1,2,2,80,128]{4,3,2,1,0:T(8,128)(2,1)} %copy-done.15) | copy-start | bytes 245764
  212.5 10.9 %copy-start.24 = (bf16[128,160]{0,1:T(8,128)(2,1)S(1)}, bf16[128,160]{0,1:T(8,128)(2,1)}, u32[]{:S(2)}) copy-start(bf16[128,160]{0,1:T(8,128)(2,1)} %convolution_convert_fusion.4) | copy-start | bytes 122884
  212.5 10.9 %copy-start.21 = (bf16[1,2,2,80,128]{4,3,2,1,0:T(8,128)(2,1)S(1)}, bf16[1,2,2,80,128]{4,3,2,1,0:T(8,128)(2,1)}, u32[]{:S(2)}) copy-start(bf16[1,2,2,80,128]{4,3,2,1,0:T(8,128)(2,1)} %copy-done.20) | copy-start | bytes 245764
  223.4 17.8 %copy-start.17 = (bf16[1,2,2,80,128]{4,3,2,1,0:T(8,128)(2,1)}, bf16[1,2,2,80,128]{4,3,2,1,0:T(8,128)(2,1)S(1)}, u32[]{:S(2)}) copy-start(bf16[1,2,2,80,128]{4,3,2,1,0:T(8,128)(2,1)S(1)} %select_dynamic-update-slice_fusion.4) | copy-start | bytes 245764
  223.5 17.7 %copy-start.22 = (bf16[1,2,2,80,128]{4,3,2,1,0:T(8,128)(2,1)}, bf16[1,2,2,80,128]{4,3,2,1,0:T(8,128)(2,1)S(1)}, u32[]{:S(2)}) copy-start(bf16[1,2,2,80,128]{4,3,2,1,0:T(8,128)(2,1)S(1)} %select_dynamic-update-slice_fusion.2) | copy-start | bytes 245764
  (15 other events, 42.8 us)
Sparse Core Ops, SparseCore 0:
  223.5 15.9 all-reduce.1
